TPU v7x, 128 devices: a whole 4x4x4 slice. The times are simulated.
128 devices in a mesh: hot: 4 (over z), dom: 32 (over y, x, core).
Axes of the slice: x: 4, y: 4, z: 4, core: 2. Of those that a mesh axis runs over, the one named last changes fastest.
Arguments:
- macro_adjoint: float32 [16, 6], P('hot'), may hold values from -6 to 6
- slip_code: int32 [32, 64, 4096], P('hot', 'dom'), may hold values from 0 to 4095
- grain_id: int32 [32, 64, 4096], P('hot', 'dom'), may hold values from 0 to 63
- grain_modulus: float32 [64], replicated, may hold values from 0.5 to 4
- slip_softening: float32 [64, 12], replicated, may hold values from 0.1 to 1.5
- rve_spot: int32 [32], P('hot'), may hold values from 0 to 15, as said below
Outputs:
- sensitivity: float32 [16, 6], P('hot')
- adjoint_field: float32 [32, 3, 64, 4096], P('hot', None, 'dom')
Inputs may be any that keep to these rules, and one draw needn't show every extreme that they name: `rve_spot`: every hot-spot is named by exactly 2 RVEs.
All inputs are finite; a program needn't handle non-finite values.
Results may differ from a plain program's by a relative error of at most 0.0003.
Values sent between devices are 32-bit elements; how exact they have to be, the bound alone decides.
No kernel may reach another device: no remote copies, remote signals or barrier semaphores. Data moves between devices by JAX's collectives and lax.ppermute only.
A program may use at most 64 MiB of HBM per device.

v0:
```python
import jax
import jax.numpy as jnp
from jax import lax
from jax.sharding import PartitionSpec as P

RES = 64
SLIPS = 12
GRAINS = 64
ITERS = 8
mass_term = 0.02


def padded_2(value, sides, width):
    for axis, dim in sides:
        devices, length = (lax.axis_size(axis), value.shape[dim])
        up = [(i, (i + 1) % devices) for i in range(devices - 1)]
        down = [(j, i) for i, j in up]
        last = lax.slice_in_dim(value, length - width, length, axis=dim)
        leading = lax.slice_in_dim(value, 0, width, axis=dim)
        before = lax.ppermute(last, axis, up)
        after = lax.ppermute(leading, axis, down)
        value = jnp.concatenate([before, value, after], axis=dim)
    return value


def shift_cells(field, step):
    filler = jnp.zeros(field.shape[:-1] + (abs(step),), field.dtype)
    if step > 0:
        return jnp.concatenate([field[..., step:], filler], -1)
    return jnp.concatenate([filler, field[..., :step]], -1)


def local_dot(first, second):
    return jnp.sum(first * second, axis=(1, 2, 3))


def shards(macro_adjoint, slip_code, grain_id, grain_modulus, slip_softening, rve_spot):
    rve_count = slip_code.shape[0]
    cells = slip_code.shape[2]
    spot_count = macro_adjoint.shape[0] * lax.axis_size("hot")
    column = jnp.arange(cells) % RES
    upper_mask = (column != RES - 1).astype(jnp.float32)
    lower_mask = (column != 0).astype(jnp.float32)
    table = jnp.concatenate([grain_modulus[None, :], slip_softening.T], 0)

    def stiff_one(inputs):
        codes, grain_cells = inputs
        flat_codes = codes.reshape(-1)
        flat_grains = grain_cells.reshape(-1)
        onehot = (jnp.arange(GRAINS)[:, None] == flat_grains[None, :]).astype(jnp.float32)
        looked = jnp.dot(
            table, onehot, precision=lax.Precision.HIGHEST, preferred_element_type=jnp.float32
        )
        softening = jnp.zeros(flat_codes.shape, jnp.float32)
        for slip in range(SLIPS):
            active = (flat_codes // 2**slip % 2).astype(jnp.float32)
            softening = softening + active * looked[1 + slip]
        return (looked[0] / (1.0 + softening)).reshape(codes.shape)

    all_strains = lax.all_gather(macro_adjoint, "hot", axis=0, tiled=True)
    spot_onehot = (rve_spot[:, None] == jnp.arange(spot_count)[None, :]).astype(jnp.float32)
    strains = jnp.dot(
        spot_onehot,
        all_strains,
        precision=lax.Precision.HIGHEST,
        preferred_element_type=jnp.float32,
    )
    stiff = lax.map(stiff_one, (slip_code, grain_id))
    padded = padded_2(stiff, (("dom", 1),), 1)

    def squares(residual):
        return lax.psum(local_dot(residual, residual), "dom")

    near_xup = padded[:, 2:]
    near_xdn = padded[:, :-2]
    near_yup = shift_cells(stiff, RES)
    near_ydn = shift_cells(stiff, -RES)
    near_zup = shift_cells(stiff, 1) * upper_mask
    near_zdn = shift_cells(stiff, -1) * lower_mask
    face_xup = 0.5 * (stiff + near_xup)
    face_xdn = 0.5 * (stiff + near_xdn)
    face_yup = 0.5 * (stiff + near_yup)
    face_ydn = 0.5 * (stiff + near_ydn)
    face_zup = 0.5 * (stiff + near_zup)
    face_zdn = 0.5 * (stiff + near_zdn)
    diagonal_sum = (mass_term + face_xup + face_xdn + face_yup + face_ydn + face_zup + face_zdn)[
        :, None
    ]
    gradients = [
        0.5 * (near_xup - near_xdn),
        0.5 * (near_yup - near_ydn),
        0.5 * (near_zup - near_zdn),
    ]
    tensor = [
        [strains[:, 0], strains[:, 5], strains[:, 4]],
        [strains[:, 5], strains[:, 1], strains[:, 3]],
        [strains[:, 4], strains[:, 3], strains[:, 2]],
    ]
    source = jnp.stack(
        [
            gradients[0] * tensor[comp][0][:, None, None]
            + gradients[1] * tensor[comp][1][:, None, None]
            + gradients[2] * tensor[comp][2][:, None, None]
            for comp in range(3)
        ],
        1,
    )

    def expand(values):
        return values[:, None, None, None]

    answer = jnp.zeros_like(source)
    residual = source
    direction = source
    norm_now = squares(residual)
    for step in range(ITERS):
        wide = padded_2(direction, (("dom", 2),), 1)
        image = (
            diagonal_sum * direction
            - face_xup[:, None] * wide[:, :, 2:]
            - face_xdn[:, None] * wide[:, :, :-2]
            - face_yup[:, None] * shift_cells(direction, RES)
            - face_ydn[:, None] * shift_cells(direction, -RES)
            - face_zup[:, None] * (shift_cells(direction, 1) * upper_mask)
            - face_zdn[:, None] * (shift_cells(direction, -1) * lower_mask)
        )
        alpha = norm_now / lax.psum(local_dot(direction, image), "dom")
        answer = answer + expand(alpha) * direction
        residual = residual - expand(alpha) * image
        norm_next = squares(residual)
        direction = residual + expand(norm_next / norm_now) * direction
        norm_now = norm_next
    volume = float(RES**3)
    stiff_part = jnp.sum(stiff, axis=(1, 2)) / volume
    moment = [
        [jnp.sum(answer[:, comp] * gradients[other], axis=(1, 2)) for other in range(3)]
        for comp in range(3)
    ]
    pairs = [(0, 0), (1, 1), (2, 2), (1, 2), (0, 2), (0, 1)]
    partial_here = jnp.stack(
        [
            stiff_part * strains[:, slot]
            - 0.5
            * (moment[pairs[slot][0]][pairs[slot][1]] + moment[pairs[slot][1]][pairs[slot][0]])
            / volume
            for slot in range(6)
        ],
        1,
    )
    per_spot = float(rve_count * lax.axis_size("hot") // spot_count)
    rve_totals = lax.psum(partial_here, "dom")
    spot_local = jnp.dot(
        spot_onehot.T,
        rve_totals,
        precision=lax.Precision.HIGHEST,
        preferred_element_type=jnp.float32,
    )
    owned = lax.psum_scatter(spot_local, "hot", scatter_dimension=0, tiled=True)
    return (owned / per_spot, answer)


def solution(mesh):
    return jax.shard_map(
        shards,
        mesh=mesh,
        in_specs=(P("hot", None), P("hot", "dom", None), P("hot", "dom", None), P(), P(), P("hot")),
        out_specs=(P("hot", None), P("hot", None, "dom", None)),
        check_vma=False,
    )
```

profile of v0, /device:TPU:0, one launch (start us, length us, event | category | flops | bytes accessed | tf_op | source)
XLA Modules:
  0.0 1254.9 jit_solution(1973612798460784764)
XLA Ops:
  1.3 40.5 %while.13 = (s32[]{:T(128)}, f32[8,2,4096]{2,1,0:T(2,128)S(1)}, s32[8,2,4096]{2,1,0:T(2,128)}, f32[13,64]{1,0:T(8,128)S(1)}, s32[8,2,4096]{2,1,0:T(2,128)}, /*index=5*/s32[]{:T(128)}) while((s32[]{:T(128)}, f32[8,2,4096]{2,1,0:T(2,128)S(1)}, s32[8,2,4096]{2,1,0:T(2,128)}, f32[13,64]{1,0:T(8,128)S(1)}, s32[8,2,4096]{2,1,0:T(2,128)}, ...), condition=%wide.region_1.2_spmd, body=%wide.region_0.1_spmd.sunk | while | flops 84582400 | bytes 2788685 | solution.py:68
  47.5 12.1 all-gather
  71.3 5.7 multiply_reduce_fusion.14
  77.0 67.4 %all-reduce.37 = (f32[8]{0:T(128)S(1)}, f32[8]{0:T(128)S(1)}) all-reduce(f32[8]{0:T(128)S(1)} %get-tuple-element.148, f32[8]{0:T(128)S(1)} %get-tuple-element.147), channel_id=1, replica_groups=mesh['hot'=4,'dom'=32] {'dom'}, use_global_device_ids=true, to_apply=%region_4.5 | all-reduce | flops 16 | bytes 128 | tf_op jit(solution)/shard_map/psum | solution.py:72
  146.3 62.9 %psum.121 = f32[8]{0:T(128)S(1)} all-reduce(f32[8]{0:T(128)S(1)} %get-tuple-element.185), channel_id=1, replica_groups=mesh['hot'=4,'dom'=32] {'dom'}, use_global_device_ids=true, to_apply=%region_8.9 | all-reduce | flops 8 | bytes 64 | tf_op jit(solution)/shard_map/psum | solution.py:72
  223.8 66.8 %psum.122 = f32[8]{0:T(128)S(1)} all-reduce(f32[8]{0:T(128)S(1)} %get-tuple-element.183), channel_id=1, replica_groups=mesh['hot'=4,'dom'=32] {'dom'}, use_global_device_ids=true, to_apply=%region_10.11 | all-reduce | flops 8 | bytes 64 | tf_op jit(solution)/shard_map/psum | solution.py:127
  293.4 62.7 %psum.123 = f32[8]{0:T(128)S(1)} all-reduce(f32[8]{0:T(128)S(1)} %get-tuple-element.181), channel_id=1, replica_groups=mesh['hot'=4,'dom'=32] {'dom'}, use_global_device_ids=true, to_apply=%region_12.13 | all-reduce | flops 8 | bytes 64 | tf_op jit(solution)/shard_map/psum | solution.py:72
  371.2 67.1 %psum.124 = f32[8]{0:T(128)S(1)} all-reduce(f32[8]{0:T(128)S(1)} %get-tuple-element.179), channel_id=1, replica_groups=mesh['hot'=4,'dom'=32] {'dom'}, use_global_device_ids=true, to_apply=%region_14.15 | all-reduce | flops 8 | bytes 64 | tf_op jit(solution)/shard_map/psum | solution.py:127
  440.9 62.7 %psum.125 = f32[8]{0:T(128)S(1)} all-reduce(f32[8]{0:T(128)S(1)} %get-tuple-element.177), channel_id=1, replica_groups=mesh['hot'=4,'dom'=32] {'dom'}, use_global_device_ids=true, to_apply=%region_16.17 | all-reduce | flops 8 | bytes 64 | tf_op jit(solution)/shard_map/psum | solution.py:72
  512.6 5.4 multiply_reduce_fusion.8
  518.1 67.1 %psum.126 = f32[8]{0:T(128)S(1)} all-reduce(f32[8]{0:T(128)S(1)} %get-tuple-element.175), channel_id=1, replica_groups=mesh['hot'=4,'dom'=32] {'dom'}, use_global_device_ids=true, to_apply=%region_18.19 | all-reduce | flops 8 | bytes 64 | tf_op jit(solution)/shard_map/psum | solution.py:127
  588.0 62.7 %psum.127 = f32[8]{0:T(128)S(1)} all-reduce(f32[8]{0:T(128)S(1)} %get-tuple-element.173), channel_id=1, replica_groups=mesh['hot'=4,'dom'=32] {'dom'}, use_global_device_ids=true, to_apply=%region_20.21 | all-reduce | flops 8 | bytes 64 | tf_op jit(solution)/shard_map/psum | solution.py:72
  660.0 5.5 multiply_reduce_fusion.6
  665.5 67.1 %psum.128 = f32[8]{0:T(128)S(1)} all-reduce(f32[8]{0:T(128)S(1)} %get-tuple-element.171), channel_id=1, replica_groups=mesh['hot'=4,'dom'=32] {'dom'}, use_global_device_ids=true, to_apply=%region_22.23 | all-reduce | flops 8 | bytes 64 | tf_op jit(solution)/shard_map/psum | solution.py:127
  735.4 62.7 %psum.129 = f32[8]{0:T(128)S(1)} all-reduce(f32[8]{0:T(128)S(1)} %get-tuple-element.169), channel_id=1, replica_groups=mesh['hot'=4,'dom'=32] {'dom'}, use_global_device_ids=true, to_apply=%region_24.25 | all-reduce | flops 8 | bytes 64 | tf_op jit(solution)/shard_map/psum | solution.py:72
  807.4 5.5 multiply_reduce_fusion.4
  812.9 67.1 %psum.130 = f32[8]{0:T(128)S(1)} all-reduce(f32[8]{0:T(128)S(1)} %get-tuple-element.167), channel_id=1, replica_groups=mesh['hot'=4,'dom'=32] {'dom'}, use_global_device_ids=true, to_apply=%region_26.27 | all-reduce | flops 8 | bytes 64 | tf_op jit(solution)/shard_map/psum | solution.py:127
  882.8 62.7 %psum.131 = f32[8]{0:T(128)S(1)} all-reduce(f32[8]{0:T(128)S(1)} %get-tuple-element.165), channel_id=1, replica_groups=mesh['hot'=4,'dom'=32] {'dom'}, use_global_device_ids=true, to_apply=%region_28.29 | all-reduce | flops 8 | bytes 64 | tf_op jit(solution)/shard_map/psum | solution.py:72
  954.8 5.5 multiply_reduce_fusion.2
  960.4 67.1 %psum.132 = f32[8]{0:T(128)S(1)} all-reduce(f32[8]{0:T(128)S(1)} %get-tuple-element.163), channel_id=1, replica_groups=mesh['hot'=4,'dom'=32] {'dom'}, use_global_device_ids=true, to_apply=%region_30.31 | all-reduce | flops 8 | bytes 64 | tf_op jit(solution)/shard_map/psum | solution.py:127
  1030.3 62.7 %psum.133 = f32[8]{0:T(128)S(1)} all-reduce(f32[8]{0:T(128)S(1)} %get-tuple-element.161), channel_id=1, replica_groups=mesh['hot'=4,'dom'=32] {'dom'}, use_global_device_ids=true, to_apply=%region_32.33 | all-reduce | flops 8 | bytes 64 | tf_op jit(solution)/shard_map/psum | solution.py:72
  1110.7 67.1 %psum.134 = f32[8]{0:T(128)S(1)} all-reduce(f32[8]{0:T(128)S(1)} %multiply_reduce_fusion), channel_id=1, replica_groups=mesh['hot'=4,'dom'=32] {'dom'}, use_global_device_ids=true, to_apply=%region_34.35 | all-reduce | flops 8 | bytes 64 | tf_op jit(solution)/shard_map/psum | solution.py:127
  1181.1 62.7 %psum.135 = f32[8,6]{0,1:T(8,128)S(1)} all-reduce(f32[8,6]{0,1:T(8,128)S(1)} %stack.25), channel_id=1, replica_groups=mesh['hot'=4,'dom'=32] {'dom'}, use_global_device_ids=true, to_apply=%region_44.45 | all-reduce | flops 48 | bytes 384 | tf_op jit(solution)/shard_map/psum | solution.py:151
  1244.1 10.0 all-reduce.36
  (375 shorter events, 163.1 us)
Async XLA Ops:
  42.1 18.4 %collective-permute-start = (f32[8,1,4096]{2,1,0:T(1,128)S(1)}, f32[8,1,4096]{2,1,0:T(1,128)S(1)}, u32[]{:S(2)}, u32[]{:S(2)}) collective-permute-start(f32[8,1,4096]{2,1,0:T(1,128)S(1)} %get-tuple-element.256), channel_id=1, source_target_pairs={{1,0},{2,1},{3,2},{4,3},{5,4},{6,5},{7,6},{8,7},{9,8},{10,9},{11,1... | collective-permute-start | bytes 393224 | tf_op jit(solution)/shard_map/ppermute | solution.py:21
  43.4 17.1 %collective-permute-start.1 = (f32[8,1,4096]{2,1,0:T(1,128)S(1)}, f32[8,1,4096]{2,1,0:T(1,128)S(1)}, u32[]{:S(2)}, u32[]{:S(2)}) collective-permute-start(f32[8,1,4096]{2,1,0:T(1,128)S(1)} %get-tuple-element.257), channel_id=1, source_target_pairs={{0,1},{1,2},{2,3},{3,4},{4,5},{5,6},{6,7},{7,8},{8,9},{9,10},{10,1... | collective-permute-start | bytes 393224 | tf_op jit(solution)/shard_map/ppermute | solution.py:20
  65.2 6.0 collective-permute-start.2
  66.5 4.7 collective-permute-start.3
  71.2 441.4 %copy-start.14 = (f32[8,2,4096]{2,1,0:T(2,128)}, f32[8,2,4096]{2,1,0:T(2,128)S(1)}, u32[]{:S(2)}) copy-start(f32[8,2,4096]{2,1,0:T(2,128)S(1)} %get-tuple-element.192) | copy-start | bytes 786436
  71.2 441.4 %copy-start.19 = (f32[8,2,4096]{2,1,0:T(2,128)}, f32[8,2,4096]{2,1,0:T(2,128)S(1)}, u32[]{:S(2)}) copy-start(f32[8,2,4096]{2,1,0:T(2,128)S(1)} %get-tuple-element.193) | copy-start | bytes 786436
  71.2 441.4 %copy-start.24 = (f32[8,2,4096]{2,1,0:T(2,128)}, f32[8,2,4096]{2,1,0:T(2,128)S(1)}, u32[]{:S(2)}) copy-start(f32[8,2,4096]{2,1,0:T(2,128)S(1)} %get-tuple-element.194) | copy-start | bytes 786436
  71.2 588.7 %copy-start.2 = (f32[8,2,4096]{2,1,0:T(2,128)}, f32[8,2,4096]{2,1,0:T(2,128)S(1)}, u32[]{:S(2)}) copy-start(f32[8,2,4096]{2,1,0:T(2,128)S(1)} %get-tuple-element.189) | copy-start | bytes 786436
  71.2 588.7 %copy-start.6 = (f32[8,2,4096]{2,1,0:T(2,128)}, f32[8,2,4096]{2,1,0:T(2,128)S(1)}, u32[]{:S(2)}) copy-start(f32[8,2,4096]{2,1,0:T(2,128)S(1)} %get-tuple-element.190) | copy-start | bytes 786436
  71.2 588.7 %copy-start.10 = (f32[8,2,4096]{2,1,0:T(2,128)}, f32[8,2,4096]{2,1,0:T(2,128)S(1)}, u32[]{:S(2)}) copy-start(f32[8,2,4096]{2,1,0:T(2,128)S(1)} %get-tuple-element.191) | copy-start | bytes 786436
  212.8 5.3 collective-permute-start.4
  214.1 4.4 collective-permute-start.5
  360.1 5.5 collective-permute-start.6
  361.4 4.4 collective-permute-start.7
  507.0 5.3 collective-permute-start.8
  508.3 4.4 collective-permute-start.9
  654.1 5.8 collective-permute-start.10
  655.4 4.5 collective-permute-start.11
  801.5 5.5 collective-permute-start.12
  802.8 4.5 collective-permute-start.13
  948.9 5.6 collective-permute-start.14
  950.3 4.5 collective-permute-start.15
  1099.9 5.5 collective-permute-start.16
  1101.3 4.5 collective-permute-start.17
  (54 other events, 972.8 us)
where the time goes:
time: 1260 us; the launch traced here: 1250 us
  blocking collectives  1060 us (84%)
  other arithmetic  101 us (8%)
  starting transfers between devices  40.6 us (3%)
  local copies, waits for them, and re-layouts  40.4 us (3%)
    psum x8, blocking collectives, squares(): return lax.psum(local_dot(residual, residual), 'dom')  506 us
    psum x7, blocking collectives, shards(): alpha = norm_now / lax.psum(local_dot(direction, image), 'dom')  470 us
    psum x1, blocking collectives, shards(): rve_totals = lax.psum(partial_here, 'dom')  62.7 us
    reduce_sum x15, other arithmetic, local_dot(): return jnp.sum(first * second, axis=(1, 2, 3))  61.2 us
    ppermute x9, starting transfers between devices, padded_2(): before = lax.ppermute(last, axis, up)  29 us
  transfers between devices with their start and end apart: 18, of which 6 were waited for; matrix products, arithmetic and copies ran while one was open for 1% of the time, Pallas kernels for 0%

commit v1 on v0

--- a/solution.py
+++ b/solution.py
@@ -148,7 +148,11 @@
         1,
     )
     per_spot = float(rve_count * lax.axis_size("hot") // spot_count)
-    rve_totals = lax.psum(partial_here, "dom")
+    rve_totals = partial_here
+    for hop in (1, 2, 4, 8, 16):
+        rve_totals = rve_totals + lax.ppermute(
+            rve_totals, "dom", [(dev, dev ^ hop) for dev in range(32)]
+        )
     spot_local = jnp.dot(
         spot_onehot.T,
         rve_totals,

time: 1260 us -> 1220 us (0.968)
  blocking collectives: 1060 us -> 998 us
  waiting for transfers between devices: 2.06 us -> 19.3 us
    psum x1 -> x0, blocking collectives: 62.7 us -> none  [shards(): rve_totals = lax.psum(partial_here, 'dom')]
    ppermute x0 -> x5, waiting for transfers between devices: none -> 17.3 us  [shards(): lax.ppermute(rve_totals, 'dom', [(dev, dev ^ hop) for dev in range(32)])]
  transfers between devices with their start and end apart: 18 -> 23, of which waited for: 6 -> 11; matrix products, arithmetic and copies ran while one was open for 1% -> 1% of each run, Pallas kernels for 0% -> 0%
where the time goes in v1:
time: 1220 us; the launch traced here: 1210 us
  blocking collectives  998 us (82%)
  other arithmetic  102 us (8%)
  local copies, waits for them, and re-layouts  40.9 us (3%)
  starting transfers between devices  40.7 us (3%)
  waiting for transfers between devices  19.3 us (2%)
    psum x8, blocking collectives, squares(): return lax.psum(local_dot(residual, residual), 'dom')  506 us
    psum x7, blocking collectives, shards(): alpha = norm_now / lax.psum(local_dot(direction, image), 'dom')  469 us
    reduce_sum x15, other arithmetic, local_dot(): return jnp.sum(first * second, axis=(1, 2, 3))  61.2 us
    ppermute x9, starting transfers between devices, padded_2(): before = lax.ppermute(last, axis, up)  29 us
  transfers between devices with their start and end apart: 23, of which 11 were waited for; matrix products, arithmetic and copies ran while one was open for 1% of the time, Pallas kernels for 0%

profile of v1, /device:TPU:0, one launch (start us, length us, event | category | flops | bytes accessed | tf_op | source)
XLA Modules:
  0.0 1211.1 jit_solution(14328796265763914335)
XLA Ops:
  1.3 40.5 %while.13 = (s32[]{:T(128)}, f32[8,2,4096]{2,1,0:T(2,128)S(1)}, s32[8,2,4096]{2,1,0:T(2,128)}, f32[13,64]{1,0:T(8,128)S(1)}, s32[8,2,4096]{2,1,0:T(2,128)}, /*index=5*/s32[]{:T(128)}) while((s32[]{:T(128)}, f32[8,2,4096]{2,1,0:T(2,128)S(1)}, s32[8,2,4096]{2,1,0:T(2,128)}, f32[13,64]{1,0:T(8,128)S(1)}, s32[8,2,4096]{2,1,0:T(2,128)}, ...), condition=%wide.region_1.2_spmd, body=%wide.region_0.1_spmd.sunk | while | flops 84582400 | bytes 2788685 | solution.py:68
  47.4 12.1 all-gather
  71.0 5.7 multiply_reduce_fusion.14
  76.7 67.5 %all-reduce.37 = (f32[8]{0:T(128)S(1)}, f32[8]{0:T(128)S(1)}) all-reduce(f32[8]{0:T(128)S(1)} %get-tuple-element.148, f32[8]{0:T(128)S(1)} %get-tuple-element.147), channel_id=1, replica_groups=mesh['hot'=4,'dom'=32] {'dom'}, use_global_device_ids=true, to_apply=%region_4.5 | all-reduce | flops 16 | bytes 128 | tf_op jit(solution)/shard_map/psum | solution.py:72
  146.3 62.9 %psum.114 = f32[8]{0:T(128)S(1)} all-reduce(f32[8]{0:T(128)S(1)} %get-tuple-element.185), channel_id=1, replica_groups=mesh['hot'=4,'dom'=32] {'dom'}, use_global_device_ids=true, to_apply=%region_8.9 | all-reduce | flops 8 | bytes 64 | tf_op jit(solution)/shard_map/psum | solution.py:72
  224.0 66.8 %psum.115 = f32[8]{0:T(128)S(1)} all-reduce(f32[8]{0:T(128)S(1)} %get-tuple-element.183), channel_id=1, replica_groups=mesh['hot'=4,'dom'=32] {'dom'}, use_global_device_ids=true, to_apply=%region_10.11 | all-reduce | flops 8 | bytes 64 | tf_op jit(solution)/shard_map/psum | solution.py:127
  293.4 62.7 %psum.116 = f32[8]{0:T(128)S(1)} all-reduce(f32[8]{0:T(128)S(1)} %get-tuple-element.181), channel_id=1, replica_groups=mesh['hot'=4,'dom'=32] {'dom'}, use_global_device_ids=true, to_apply=%region_12.13 | all-reduce | flops 8 | bytes 64 | tf_op jit(solution)/shard_map/psum | solution.py:72
  366.0 5.4 multiply_reduce_fusion.10
  371.4 67.1 %psum.117 = f32[8]{0:T(128)S(1)} all-reduce(f32[8]{0:T(128)S(1)} %get-tuple-element.179), channel_id=1, replica_groups=mesh['hot'=4,'dom'=32] {'dom'}, use_global_device_ids=true, to_apply=%region_14.15 | all-reduce | flops 8 | bytes 64 | tf_op jit(solution)/shard_map/psum | solution.py:127
  441.1 62.7 %psum.118 = f32[8]{0:T(128)S(1)} all-reduce(f32[8]{0:T(128)S(1)} %get-tuple-element.177), channel_id=1, replica_groups=mesh['hot'=4,'dom'=32] {'dom'}, use_global_device_ids=true, to_apply=%region_16.17 | all-reduce | flops 8 | bytes 64 | tf_op jit(solution)/shard_map/psum | solution.py:72
  513.0 5.4 multiply_reduce_fusion.8
  518.5 67.1 %psum.119 = f32[8]{0:T(128)S(1)} all-reduce(f32[8]{0:T(128)S(1)} %get-tuple-element.175), channel_id=1, replica_groups=mesh['hot'=4,'dom'=32] {'dom'}, use_global_device_ids=true, to_apply=%region_18.19 | all-reduce | flops 8 | bytes 64 | tf_op jit(solution)/shard_map/psum | solution.py:127
  588.4 62.7 %psum.120 = f32[8]{0:T(128)S(1)} all-reduce(f32[8]{0:T(128)S(1)} %get-tuple-element.173), channel_id=1, replica_groups=mesh['hot'=4,'dom'=32] {'dom'}, use_global_device_ids=true, to_apply=%region_20.21 | all-reduce | flops 8 | bytes 64 | tf_op jit(solution)/shard_map/psum | solution.py:72
  660.6 5.5 multiply_reduce_fusion.6
  666.0 67.1 %psum.121 = f32[8]{0:T(128)S(1)} all-reduce(f32[8]{0:T(128)S(1)} %get-tuple-element.171), channel_id=1, replica_groups=mesh['hot'=4,'dom'=32] {'dom'}, use_global_device_ids=true, to_apply=%region_22.23 | all-reduce | flops 8 | bytes 64 | tf_op jit(solution)/shard_map/psum | solution.py:127
  735.9 62.7 %psum.122 = f32[8]{0:T(128)S(1)} all-reduce(f32[8]{0:T(128)S(1)} %get-tuple-element.169), channel_id=1, replica_groups=mesh['hot'=4,'dom'=32] {'dom'}, use_global_device_ids=true, to_apply=%region_24.25 | all-reduce | flops 8 | bytes 64 | tf_op jit(solution)/shard_map/psum | solution.py:72
  808.1 5.5 multiply_reduce_fusion.4
  813.6 67.1 %psum.123 = f32[8]{0:T(128)S(1)} all-reduce(f32[8]{0:T(128)S(1)} %get-tuple-element.167), channel_id=1, replica_groups=mesh['hot'=4,'dom'=32] {'dom'}, use_global_device_ids=true, to_apply=%region_26.27 | all-reduce | flops 8 | bytes 64 | tf_op jit(solution)/shard_map/psum | solution.py:127
  883.5 62.7 %psum.124 = f32[8]{0:T(128)S(1)} all-reduce(f32[8]{0:T(128)S(1)} %get-tuple-element.165), channel_id=1, replica_groups=mesh['hot'=4,'dom'=32] {'dom'}, use_global_device_ids=true, to_apply=%region_28.29 | all-reduce | flops 8 | bytes 64 | tf_op jit(solution)/shard_map/psum | solution.py:72
  955.5 5.5 multiply_reduce_fusion.2
  961.0 67.1 %psum.125 = f32[8]{0:T(128)S(1)} all-reduce(f32[8]{0:T(128)S(1)} %get-tuple-element.163), channel_id=1, replica_groups=mesh['hot'=4,'dom'=32] {'dom'}, use_global_device_ids=true, to_apply=%region_30.31 | all-reduce | flops 8 | bytes 64 | tf_op jit(solution)/shard_map/psum | solution.py:127
  1031.0 62.7 %psum.126 = f32[8]{0:T(128)S(1)} all-reduce(f32[8]{0:T(128)S(1)} %get-tuple-element.161), channel_id=1, replica_groups=mesh['hot'=4,'dom'=32] {'dom'}, use_global_device_ids=true, to_apply=%region_32.33 | all-reduce | flops 8 | bytes 64 | tf_op jit(solution)/shard_map/psum | solution.py:72
  1110.8 67.1 %psum.127 = f32[8]{0:T(128)S(1)} all-reduce(f32[8]{0:T(128)S(1)} %multiply_reduce_fusion), channel_id=1, replica_groups=mesh['hot'=4,'dom'=32] {'dom'}, use_global_device_ids=true, to_apply=%region_34.35 | all-reduce | flops 8 | bytes 64 | tf_op jit(solution)/shard_map/psum | solution.py:127
  1200.3 10.0 all-reduce.36
  (358 shorter events, 176.8 us)
Async XLA Ops:
  42.1 17.7 %collective-permute-start = (f32[8,1,4096]{2,1,0:T(1,128)S(1)}, f32[8,1,4096]{2,1,0:T(1,128)S(1)}, u32[]{:S(2)}, u32[]{:S(2)}) collective-permute-start(f32[8,1,4096]{2,1,0:T(1,128)S(1)} %get-tuple-element.256), channel_id=1, source_target_pairs={{1,0},{2,1},{3,2},{4,3},{5,4},{6,5},{7,6},{8,7},{9,8},{10,9},{11,1... | collective-permute-start | bytes 393224 | tf_op jit(solution)/shard_map/ppermute | solution.py:21
  43.4 16.4 %collective-permute-start.1 = (f32[8,1,4096]{2,1,0:T(1,128)S(1)}, f32[8,1,4096]{2,1,0:T(1,128)S(1)}, u32[]{:S(2)}, u32[]{:S(2)}) collective-permute-start(f32[8,1,4096]{2,1,0:T(1,128)S(1)} %get-tuple-element.257), channel_id=1, source_target_pairs={{0,1},{1,2},{2,3},{3,4},{4,5},{5,6},{6,7},{7,8},{8,9},{9,10},{10,1... | collective-permute-start | bytes 393224 | tf_op jit(solution)/shard_map/ppermute | solution.py:20
  65.1 5.9 collective-permute-start.2
  66.4 4.6 collective-permute-start.3
  71.0 589.5 %copy-start.2 = (f32[8,2,4096]{2,1,0:T(2,128)}, f32[8,2,4096]{2,1,0:T(2,128)S(1)}, u32[]{:S(2)}) copy-start(f32[8,2,4096]{2,1,0:T(2,128)S(1)} %get-tuple-element.189) | copy-start | bytes 786436
  212.9 5.3 collective-permute-start.4
  214.2 4.4 collective-permute-start.5
  360.3 5.5 collective-permute-start.6
  361.6 4.4 collective-permute-start.7
  507.3 5.3 collective-permute-start.8
  508.6 4.4 collective-permute-start.9
  654.6 5.8 collective-permute-start.10
  656.0 4.5 collective-permute-start.11
  802.2 5.5 collective-permute-start.12
  803.5 4.5 collective-permute-start.13
  949.6 5.6 collective-permute-start.14
  951.0 4.5 collective-permute-start.15
  1100.7 5.5 collective-permute-start.16
  1102.0 4.5 collective-permute-start.17
  1181.3 1.2 collective-permute-start.18
  1182.6 3.6 collective-permute-start.19
  1186.2 5.1 collective-permute-start.20
  1191.3 3.6 collective-permute-start.21
  1194.9 5.1 collective-permute-start.22
  (44 other events, 3106.9 us)
